TPU v7x, 128 devices: a whole 4x4x4 slice. The times are simulated.
128 devices in a mesh: tok: 8 (over z, core), wid: 16 (over y, x).
Axes of the slice: x: 4, y: 4, z: 4, core: 2. Of those that a mesh axis runs over, the one named last changes fastest.
Arguments:
- tokens: bfloat16 [8192, 3072], P('tok', 'wid'), may hold values from -6 to 6
- defect_mask: int32 [8192], P('tok'), may hold values 0 or 1
- timestep: int32 [1], replicated, may hold values from 0 to 999
- mask_embed: bfloat16 [3072], P('wid'), may hold values from -6 to 6
- mod_weight: bfloat16 [256, 3, 3072], P(None, None, 'wid'), may hold values from -0.375 to 0.375
- w_qkv: bfloat16 [3072, 3, 2048], P('tok', None, 'wid'), may hold values from -1.4614179 to 1.4614179, as said below
- w_out: bfloat16 [2048, 3072], P('wid'), may hold values from -0.125 to 0.125
Outputs:
- block_out: bfloat16 [8192, 3072], P('tok', 'wid')
Inputs may be any that keep to these rules, and one draw needn't show every extreme that they name: `w_qkv`: entries are at most 81 / sqrt(3072) in magnitude.
All inputs are finite; a program needn't handle non-finite values. No bound on the sum of `defect_mask` on one device may be relied on, other than what follows from the above.
Results may differ from a plain program's by a relative error of at most 0.011.
Values may be sent and summed in bfloat16 or wider, within the bound.
No kernel may reach another device: no remote copies, remote signals or barrier semaphores. Data moves between devices by JAX's collectives and lax.ppermute only.
A program may use at most 128 MiB of HBM per device.

v0:
```python
import math
import jax
import jax.numpy as jnp
from jax import lax
from jax.sharding import PartitionSpec as P

D = 3072
DH = 128
TEMB = 256


def finish_rows(values, row_mean, row_var, shift_row, scale_row):
    normal = (values - row_mean) * lax.rsqrt(row_var + 1e-06)
    return (normal * (1.0 + scale_row.astype(jnp.float32)) + shift_row.astype(jnp.float32)).astype(
        jnp.bfloat16
    )


def body(tokens, defect_mask, timestep, mask_embed, mod_weight, w_qkv, w_out):
    tok_rows = tokens.shape[0]
    residual_in = (
        tokens.astype(jnp.float32)
        + defect_mask.astype(jnp.float32)[:, None] * mask_embed.astype(jnp.float32)[None, :]
    ).astype(jnp.bfloat16)
    w_cols = lax.all_to_all(w_out, "wid", split_axis=1, concat_axis=0, tiled=True)
    w_full = lax.all_gather(w_qkv, "tok", axis=0, tiled=True)
    residual_full = lax.all_gather(residual_in, "wid", axis=1, tiled=True)
    half_width = TEMB // 2
    frequency = jnp.exp(-math.log(10000.0) * jnp.arange(half_width, dtype=jnp.float32) / half_width)
    angles = timestep.astype(jnp.float32)[0] * frequency
    embedding = jnp.concatenate([jnp.cos(angles), jnp.sin(angles)])
    modulation = jnp.einsum(
        "e,ecf->cf",
        jax.nn.silu(embedding),
        mod_weight.astype(jnp.float32),
        precision=lax.Precision.HIGHEST,
    ).astype(jnp.bfloat16)
    shift_scale = lax.all_gather(modulation[:2], "wid", axis=1, tiled=True)
    values = residual_full.astype(jnp.float32)
    row_mean = jnp.mean(values, axis=1, keepdims=True)
    row_var = jnp.mean(values * values, axis=1, keepdims=True) - row_mean * row_mean
    normed = finish_rows(
        values, row_mean, row_var, shift_scale[0][None, :], shift_scale[1][None, :]
    )
    qkv = jnp.einsum("td,dcf->tcf", normed, w_full, preferred_element_type=jnp.float32).astype(
        jnp.bfloat16
    )
    queries = qkv[:, 0]
    key_values = lax.all_gather(qkv[:, 1:3], "tok", axis=0, tiled=True)
    key_part = key_values[:, 0]
    value_part = key_values[:, 1]
    score_scale = DH ** (-0.5)
    scores = jnp.dot(queries, key_part.T, preferred_element_type=jnp.float32) * score_scale
    shifted = jnp.exp(scores - jnp.max(scores, axis=1, keepdims=True))
    row_sum = jnp.sum(shifted, axis=1, keepdims=True)
    numer = jnp.dot(shifted.astype(jnp.bfloat16), value_part, preferred_element_type=jnp.float32)
    attended = (numer / row_sum).astype(jnp.bfloat16)
    attended_full = lax.all_gather(attended, "wid", axis=1, tiled=True)
    projected = jnp.dot(attended_full, w_cols, preferred_element_type=jnp.float32)
    return (
        residual_in.astype(jnp.float32) + modulation[2].astype(jnp.float32)[None, :] * projected
    ).astype(jnp.bfloat16)


def solution(mesh):
    return jax.shard_map(
        body,
        mesh=mesh,
        in_specs=(
            P("tok", "wid"),
            P("tok"),
            P(),
            P("wid"),
            P(None, None, "wid"),
            P("tok", None, "wid"),
            P("wid", None),
        ),
        out_specs=P("tok", "wid"),
        check_vma=False,
    )
```

profile of v0, /device:TPU:0, one launch (start us, length us, event | category | flops | bytes accessed | tf_op | source)
XLA Modules:
  0.0 257.7 jit_solution(2055310667974810968)
XLA Ops:
  6.5 0.7 convert_element_type.47
  7.3 0.7 convert_element_type.48
  7.9 1.9 add_convert_fusion
  9.9 0.0 all-gather.8.cloned.1.call-start
  9.9 0.7 all-gather.8.cloned.1.call-update
  10.6 0.0 all-gather.10.cloned.1.call-start
  11.4 0.3 fusion.30
  11.8 23.8 %all-gather = bf16[16,192,2]{1,2,0:T(2,128)(2,1)S(1)} all-gather(bf16[1,192,2]{1,2,0:T(2,128)(2,1)S(1)} %slice_bitcast_fusion.10), channel_id=1, replica_groups=mesh['tok'=8,'wid'=16] {'wid'}, dimensions={0}, use_global_device_ids=true | all-gather | bytes 13056 | tf_op jit(solution)/shard_map/all_gather | solution.py:38
  35.6 0.1 reshape.28
  35.7 38.0 %all-gather.6.cloned.1.call-done = bf16[1024,3072]{0,1:T(8,128)(2,1)} async-done(((bf16[1024,192]{0,1:T(8,128)(2,1)}), bf16[1024,3072]{0,1:T(8,128)(2,1)}) %all-gather.6.cloned.1.call-update) | async-done | bytes 6291472 | tf_op jit(solution)/shard_map/all_gather | solution.py:27
  73.7 4.5 %convert_reduce_fusion = (f32[1024]{0:T(1024)S(1)}, f32[1024]{0:T(1024)S(1)}) fusion(bf16[1024,3072]{0,1:T(8,128)(2,1)} %all-gather.6.cloned.1.call-done), kind=kLoop, calls=%fused_computation.6 | loop fusion | flops 12580864 | bytes 6299648 | tf_op jit(solution)/shard_map/reduce_sum | solution.py:40
  78.2 22.8 %all-gather.8.cloned.1.call-done = bf16[3072,3,128]{2,0,1:T(8,128)(2,1)} async-done(((bf16[384,3,128]{2,0,1:T(8,128)(2,1)}), bf16[3072,3,128]{2,0,1:T(8,128)(2,1)}) %all-gather.8.cloned.1.call-update) | async-done | bytes 2359312 | tf_op jit(solution)/shard_map/all_gather | solution.py:26
  100.9 7.2 %fusion.13 = bf16[1024,3,128]{2,0,1:T(8,128)(2,1)S(1)} fusion(bf16[3072,3,128]{2,0,1:T(8,128)(2,1)} %all-gather.8.cloned.1.call-done, bf16[1024,3072]{0,1:T(8,128)(2,1)} %all-gather.6.cloned.1.call-done, f32[3072]{0:T(1024)S(1)} %bitcast.53, f32[3072]{0:T(1024)S(1)} %bitcast.52, f32[1024]{0:T(1024)S(1)} %get-tuple-element.8, f32[1024]{0:T(1024)S(1)} %get-tuple-element.7), kind=kOutput, calls=%fused_computation.18 | convolution fusion | flops 2435186688 | bytes 9469952 | tf_op jit(solution)/shard_map/td,dcf->tcf/dot_general | solution.py:45
  108.1 0.8 slice.37
  109.0 0.2 all-gather.12.cloned.1.call-start
  109.2 32.7 %all-gather.10.cloned.1.call-done = bf16[8192,2,128]{2,0,1:T(8,128)(2,1)} async-done(((bf16[1024,2,128]{2,0,1:T(8,128)(2,1)}), bf16[8192,2,128]{2,0,1:T(8,128)(2,1)}) %all-gather.10.cloned.1.call-update) | async-done | bytes 4194320 | tf_op jit(solution)/shard_map/all_gather | solution.py:49
  141.9 14.7 %multiply_reduce_fusion = (f32[1024]{0:T(1024)S(1)}, f32[1024,8192]{1,0:T(8,128)}) fusion(bf16[8192,2,128]{2,0,1:T(8,128)(2,1)} %all-gather.10.cloned.1.call-done, bf16[1024,3,128]{2,0,1:T(8,128)(2,1)S(1)} %fusion.13), kind=kOutput, calls=%fused_computation.1 | convolution fusion | flops 2164259840 | bytes 35917824 | tf_op jit(solution)/shard_map/dot_general | solution.py:53
  156.5 14.3 %fusion = f32[1024]{0:T(1024)S(1)} fusion(f32[1024,8192]{1,0:T(8,128)} %get-tuple-element.10, f32[1024]{0:T(1024)S(1)} %get-tuple-element.9), kind=kLoop, calls=%fused_computation.2 | loop fusion | flops 25164800 | bytes 33562624 | tf_op jit(solution)/shard_map/reduce_sum | solution.py:55
  170.8 14.2 %fusion.21 = bf16[1024,128]{1,0:T(8,128)(2,1)} fusion(bf16[8192,2,128]{2,0,1:T(8,128)(2,1)S(1)} %copy-done.2, f32[1024,8192]{1,0:T(8,128)} %get-tuple-element.10, f32[1024]{0:T(1024)S(1)} %get-tuple-element.9, f32[1024]{0:T(1024)S(1)} %fusion), kind=kOutput, calls=%fused_computation.23 | convolution fusion | flops 2172911616 | bytes 35921920 | tf_op jit(solution)/shard_map/dot_general | solution.py:56
  185.0 1.2 copy.18
  186.2 6.8 %all-to-all-start = ((bf16[128,16,192]{0,2,1:T(8,128)(2,1)}), bf16[128,16,192]{0,2,1:T(8,128)(2,1)S(1)}, u32[]{:S(2)}, u32[]{:S(2)}) async-start(bf16[128,16,192]{0,2,1:T(8,128)(2,1)} %bitcast.13), calls=%async_computation | async-start | bytes 1572864 | tf_op jit(solution)/shard_map/all_to_all | solution.py:25
  193.0 17.5 %all-to-all-done = bf16[128,16,192]{0,2,1:T(8,128)(2,1)S(1)} async-done(((bf16[128,16,192]{0,2,1:T(8,128)(2,1)}), bf16[128,16,192]{0,2,1:T(8,128)(2,1)S(1)}, u32[]{:S(2)}, u32[]{:S(2)}) %all-to-all-start) | async-done | bytes 786464 | tf_op jit(solution)/shard_map/all_to_all | solution.py:25
  210.6 36.1 %all-gather.12.cloned.1.call-done = bf16[1024,2048]{1,0:T(8,128)(2,1)} async-done(((bf16[1024,128]{1,0:T(8,128)(2,1)}), bf16[1024,2048]{1,0:T(8,128)(2,1)}) %all-gather.12.cloned.1.call-update) | async-done | bytes 4194320 | tf_op jit(solution)/shard_map/all_gather | solution.py:58
  246.7 4.5 %fusion.17 = bf16[1024,192]{0,1:T(8,128)(2,1)} fusion(bf16[1024,2048]{1,0:T(8,128)(2,1)} %all-gather.12.cloned.1.call-done, bf16[1024,192]{0,1:T(8,128)(2,1)S(1)} %copy-done.1, f32[192]{0:T(256)S(1)} %bitcast.57, bf16[128,16,192]{0,2,1:T(8,128)(2,1)S(1)} %all-to-all-done), kind=kOutput, calls=%fused_computation.21 | convolution fusion | flops 806092800 | bytes 5767936 | tf_op jit(solution)/shard_map/dot_general | solution.py:59
  (21 shorter events, 0.2 us)
Async XLA Ops:
  6.5 4.8 %copy-start = (bf16[256,3,192]{0,2,1:T(8,128)(2,1)S(1)}, bf16[256,3,192]{0,2,1:T(8,128)(2,1)}, u32[]{:S(2)}) copy-start(bf16[256,3,192]{0,2,1:T(8,128)(2,1)} %param.11) | copy-start | bytes 884740
  6.5 67.1 %all-gather.6.cloned.1.call-start = ((), (), s32[]{:S(2)}) async-start(), calls=%async_computation.1 | async-start | bytes 6684672 | tf_op jit(solution)/shard_map/all_gather | solution.py:27
  9.9 91.1 %all-gather.8.cloned.1.call-start = ((), (), s32[]{:S(2)}) async-start(), calls=%async_computation.2 | async-start | bytes 2654208 | tf_op jit(solution)/shard_map/all_gather | solution.py:26
  10.6 131.3 %all-gather.10.cloned.1.call-start = ((), (), s32[]{:S(2)}) async-start(), calls=%async_computation.3 | async-start | bytes 4718592 | tf_op jit(solution)/shard_map/all_gather | solution.py:49
  109.0 137.7 %all-gather.12.cloned.1.call-start = ((), (), s32[]{:S(2)}) async-start(), calls=%async_computation.4 | async-start | bytes 4456448 | tf_op jit(solution)/shard_map/all_gather | solution.py:58
  156.5 14.3 %copy-start.2 = (bf16[8192,2,128]{2,0,1:T(8,128)(2,1)S(1)}, bf16[8192,2,128]{2,0,1:T(8,128)(2,1)}, u32[]{:S(2)}) copy-start(bf16[8192,2,128]{2,0,1:T(8,128)(2,1)} %all-gather.10.cloned.1.call-done) | copy-start | bytes 12582916
  170.8 14.2 %copy-start.3 = (bf16[128,3072]{1,0:T(8,128)(2,1)S(1)}, bf16[128,3072]{1,0:T(8,128)(2,1)}, u32[]{:S(2)}) copy-start(bf16[128,3072]{1,0:T(8,128)(2,1)} %param.13) | copy-start | bytes 2359300
  170.8 75.8 %copy-start.1 = (bf16[1024,192]{0,1:T(8,128)(2,1)S(1)}, bf16[1024,192]{0,1:T(8,128)(2,1)}, u32[]{:S(2)}) copy-start(bf16[1024,192]{0,1:T(8,128)(2,1)} %add_convert_fusion) | copy-start | bytes 1179652
  186.2 24.4 %all-to-all-start = ((bf16[128,16,192]{0,2,1:T(8,128)(2,1)}), bf16[128,16,192]{0,2,1:T(8,128)(2,1)S(1)}, u32[]{:S(2)}, u32[]{:S(2)}) async-start(bf16[128,16,192]{0,2,1:T(8,128)(2,1)} %bitcast.13), calls=%async_computation | async-start | bytes 1572864 | tf_op jit(solution)/shard_map/all_to_all | solution.py:25
Sparse Core Ops, SparseCore 0:
  10.0 63.6 all-gather.5
  75.4 25.5 all-gather.7
  109.1 32.7 all-gather.9
  185.2 61.4 all-gather.11
where the time goes:
time: 258 us
  waiting for transfers between devices  148 us (57%)
  matrix products  40.9 us (16%)
  blocking collectives  23.8 us (9%)
  other arithmetic  22.1 us (9%)
  between operations  13.9 us (5%)
  starting transfers between devices  7.11 us (3%)
    all_gather x1, waiting for transfers between devices, body(): residual_full = lax.all_gather(residual_in, 'wid', axis=1, tiled=True)  38 us
    all_gather x1, waiting for transfers between devices, body(): attended_full = lax.all_gather(attended, 'wid', axis=1, tiled=True)  36.1 us
    all_gather x1, waiting for transfers between devices, body(): key_values = lax.all_gather(qkv[:, 1:3], 'tok', axis=0, tiled=True)  32.7 us
    all_gather x1, blocking collectives, body(): shift_scale = lax.all_gather(modulation[:2], 'wid', axis=1, tiled=True)  23.8 us
    all_gather x1, waiting for transfers between devices, body(): w_full = lax.all_gather(w_qkv, 'tok', axis=0, tiled=True)  22.8 us
    all_to_all x1, waiting for transfers between devices, body(): lax.all_to_all(w_out, 'wid', split_axis=1, concat_axis=0, tiled=True)  17.5 us
    dot_general x1, matrix products, body(): jnp.dot(queries, key_part.T, preferred_element_type=jnp.float32)  14.7 us
    reduce_sum x1, other arithmetic, body(): row_sum = jnp.sum(shifted, axis=1, keepdims=True)  14.3 us
  transfers between devices with their start and end apart: 5, of which 5 were waited for; matrix products, arithmetic and copies ran while one was open for 2% of the time, Pallas kernels for 0%

commit v1 on v0

--- a/solution.py
+++ b/solution.py
@@ -7,6 +7,24 @@
 D = 3072
 DH = 128
 TEMB = 256
+
+
+def pair_the_waves(chunk, mesh_dim, x_in):
+    prior, local_next, front = (lax.axis_size(mesh_dim), lax.axis_index(mesh_dim), chunk.shape[0])
+    all_blocks = [(ii, (ii + 1) % prior) for ii in range(prior)]
+    ready = prior // 2
+    entries = [(ii, (ii - 1) % prior) for ii in range(prior)]
+    o_now = x_in(chunk, local_next * front)
+    m = 1
+    inter = small = chunk
+    while m < ready + 1:
+        inter = lax.ppermute(inter, mesh_dim, all_blocks)
+        if m < prior - ready:
+            small = lax.ppermute(small, mesh_dim, entries)
+            o_now = o_now + x_in(small, (local_next + m) % prior * front)
+        o_now = o_now + x_in(inter, (local_next - m) % prior * front)
+        m += 1
+    return o_now
 
 
 def finish_rows(values, row_mean, row_var, shift_row, scale_row):
@@ -23,7 +41,6 @@
         + defect_mask.astype(jnp.float32)[:, None] * mask_embed.astype(jnp.float32)[None, :]
     ).astype(jnp.bfloat16)
     w_cols = lax.all_to_all(w_out, "wid", split_axis=1, concat_axis=0, tiled=True)
-    w_full = lax.all_gather(w_qkv, "tok", axis=0, tiled=True)
     residual_full = lax.all_gather(residual_in, "wid", axis=1, tiled=True)
     half_width = TEMB // 2
     frequency = jnp.exp(-math.log(10000.0) * jnp.arange(half_width, dtype=jnp.float32) / half_width)
@@ -42,9 +59,16 @@
     normed = finish_rows(
         values, row_mean, row_var, shift_scale[0][None, :], shift_scale[1][None, :]
     )
-    qkv = jnp.einsum("td,dcf->tcf", normed, w_full, preferred_element_type=jnp.float32).astype(
-        jnp.bfloat16
-    )
+    qkv = pair_the_waves(
+        w_qkv,
+        "tok",
+        lambda part, start: jnp.einsum(
+            "td,dcf->tcf",
+            lax.dynamic_slice_in_dim(normed, start, part.shape[0], axis=1),
+            part,
+            preferred_element_type=jnp.float32,
+        ),
+    ).astype(jnp.bfloat16)
     queries = qkv[:, 0]
     key_values = lax.all_gather(qkv[:, 1:3], "tok", axis=0, tiled=True)
     key_part = key_values[:, 0]

time: 258 us -> 246 us (0.953)
  waiting for transfers between devices: 148 us -> 115 us
  starting transfers between devices: 7.11 us -> 16.6 us
  local copies, waits for them, and re-layouts: 2.14 us -> 10.8 us
  other arithmetic: 22.1 us -> 26.3 us
    all_gather x1 -> x0, waiting for transfers between devices: 22.8 us -> none  [body(): w_full = lax.all_gather(w_qkv, 'tok', axis=0, tiled=True)]
    all_gather x1, waiting for transfers between devices: 38 us -> 20.4 us  [body(): residual_full = lax.all_gather(residual_in, 'wid', axis=1, tiled=True)]
    ppermute x0 -> x7, starting transfers between devices: none -> 9.54 us  [the longest x3 9.52 us: pair_the_waves(): small = lax.ppermute(small, mesh_dim, entries)]
    all_gather x0 -> x1, local copies, waits for them, and re-layouts: none -> 8.63 us  [body(): residual_full = lax.all_gather(residual_in, 'wid', axis=1, tiled=True)]
    ppermute x0 -> x7, waiting for transfers between devices: none -> 8.59 us  [the longest x4 8.58 us: pair_the_waves(): inter = lax.ppermute(inter, mesh_dim, all_blocks)]
    convert_element_type x0 -> x1, other arithmetic: none -> 3.81 us  [finish_rows(): (normal * (1.0 + scale_row.astype(jnp.float32)) + shift_row.astype(jnp.fl...]
    dot_general x1 -> x8, matrix products: 7.21 us -> 5.47 us  [body(): jnp.einsum('td,dcf->tcf', lax.dynamic_slice_in_dim(normed, start, part.sh...]
  transfers between devices with their start and end apart: 5 -> 11, of which waited for: 5 -> 6; matrix products, arithmetic and copies ran while one was open for 2% -> 10% of each run, Pallas kernels for 0% -> 0%
where the time goes in v1:
time: 246 us; the launch traced here: 245 us
  waiting for transfers between devices  115 us (47%)
  matrix products  39.2 us (16%)
  other arithmetic  26.3 us (11%)
  blocking collectives  23.7 us (10%)
  starting transfers between devices  16.6 us (7%)
  between operations  14.2 us (6%)
  local copies, waits for them, and re-layouts  10.8 us (4%)
    all_gather x1, waiting for transfers between devices, body(): attended_full = lax.all_gather(attended, 'wid', axis=1, tiled=True)  36.1 us
    all_gather x1, waiting for transfers between devices, body(): key_values = lax.all_gather(qkv[:, 1:3], 'tok', axis=0, tiled=True)  31.9 us
    all_gather x1, blocking collectives, body(): shift_scale = lax.all_gather(modulation[:2], 'wid', axis=1, tiled=True)  23.7 us
    all_gather x1, waiting for transfers between devices, body(): residual_full = lax.all_gather(residual_in, 'wid', axis=1, tiled=True)  20.4 us
    all_to_all x1, waiting for transfers between devices, body(): lax.all_to_all(w_out, 'wid', split_axis=1, concat_axis=0, tiled=True)  17.5 us
    dot_general x1, matrix products, body(): jnp.dot(queries, key_part.T, preferred_element_type=jnp.float32)  14.7 us
    reduce_sum x1, other arithmetic, body(): row_sum = jnp.sum(shifted, axis=1, keepdims=True)  14.3 us
    dot_general x1, matrix products, body(): jnp.dot(shifted.astype(jnp.bfloat16), value_part, preferred_element_type=...  14.2 us
  transfers between devices with their start and end apart: 11, of which 6 were waited for; matrix products, arithmetic and copies ran while one was open for 10% of the time, Pallas kernels for 0%

profile of v1, /device:TPU:0, one launch (start us, length us, event | category | flops | bytes accessed | tf_op | source)
XLA Modules:
  0.0 245.3 jit_solution(8006778684488986825)
XLA Ops:
  6.5 0.7 convert_element_type.47
  7.3 0.7 convert_element_type.48
  7.9 1.9 add_convert_fusion.1
  9.9 3.6 %collective-permute-start = (bf16[384,3,128]{2,0,1:T(8,128)(2,1)}, bf16[384,3,128]{2,0,1:T(8,128)(2,1)S(1)}, u32[]{:S(2)}, u32[]{:S(2)}) collective-permute-start(bf16[384,3,128]{2,0,1:T(8,128)(2,1)} %param.12), channel_id=1, source_target_pairs={{0,112},{16,0},{32,16},{48,32},{64,48},{80,64},{96,80},{112,96},{1... | collective-permute-start | bytes 884744 | tf_op jit(solution)/shard_map/ppermute | solution.py:23
  14.6 23.7 %all-gather = bf16[16,192,2]{1,2,0:T(2,128)(2,1)S(1)} all-gather(bf16[1,192,2]{1,2,0:T(2,128)(2,1)S(1)} %slice_bitcast_fusion.10), channel_id=1, replica_groups=mesh['tok'=8,'wid'=16] {'wid'}, dimensions={0}, use_global_device_ids=true | all-gather | bytes 13056 | tf_op jit(solution)/shard_map/all_gather | solution.py:55
  38.5 3.0 %collective-permute-start.2 = (bf16[384,3,128]{2,0,1:T(8,128)(2,1)S(1)}, bf16[384,3,128]{2,0,1:T(8,128)(2,1)S(1)}, u32[]{:S(2)}, u32[]{:S(2)}) collective-permute-start(bf16[384,3,128]{2,0,1:T(8,128)(2,1)S(1)} %collective-permute-done), channel_id=1, source_target_pairs={{0,112},{16,0},{32,16},{48,32},{64,48},{80,64},{96,80},{112,96},{1... | collective-permute-start | bytes 884744 | tf_op jit(solution)/shard_map/ppermute | solution.py:23
  41.5 4.4 %collective-permute-done.3 = bf16[384,3,128]{2,0,1:T(8,128)(2,1)S(1)} collective-permute-done((bf16[384,3,128]{2,0,1:T(8,128)(2,1)S(1)}, bf16[384,3,128]{2,0,1:T(8,128)(2,1)S(1)}, u32[]{:S(2)}, u32[]{:S(2)}) %collective-permute-start.3) | collective-permute-done | bytes 294944 | tf_op jit(solution)/shard_map/ppermute | solution.py:21
  46.0 3.0 %collective-permute-start.4 = (bf16[384,3,128]{2,0,1:T(8,128)(2,1)S(1)}, bf16[384,3,128]{2,0,1:T(8,128)(2,1)S(1)}, u32[]{:S(2)}, u32[]{:S(2)}) collective-permute-start(bf16[384,3,128]{2,0,1:T(8,128)(2,1)S(1)} %collective-permute-done.2), channel_id=1, source_target_pairs={{0,112},{16,0},{32,16},{48,32},{64,48},{80,64},{96,80},{112,96},{1... | collective-permute-start | bytes 884744 | tf_op jit(solution)/shard_map/ppermute | solution.py:23
  48.9 4.2 %collective-permute-done.5 = bf16[384,3,128]{2,0,1:T(8,128)(2,1)S(1)} collective-permute-done((bf16[384,3,128]{2,0,1:T(8,128)(2,1)S(1)}, bf16[384,3,128]{2,0,1:T(8,128)(2,1)S(1)}, u32[]{:S(2)}, u32[]{:S(2)}) %collective-permute-start.5) | collective-permute-done | bytes 294944 | tf_op jit(solution)/shard_map/ppermute | solution.py:21
  53.2 20.4 %all-gather.5.cloned.1.call-done = bf16[1024,3072]{0,1:T(8,128)(2,1)} async-done(((bf16[1024,192]{0,1:T(8,128)(2,1)}), bf16[1024,3072]{0,1:T(8,128)(2,1)}) %all-gather.5.cloned.1.call-update) | async-done | bytes 6291472 | tf_op jit(solution)/shard_map/all_gather | solution.py:44
  73.6 8.6 %copy.22 = bf16[1024,3072]{1,0:T(8,128)(2,1)} copy(bf16[1024,3072]{0,1:T(8,128)(2,1)} %all-gather.5.cloned.1.call-done) | data formatting | bytes 12582912 | tf_op jit(solution)/shard_map/all_gather | solution.py:44
  82.3 4.8 %convert_reduce_fusion = (f32[1024]{0:T(1024)S(1)}, f32[1024]{0:T(1024)S(1)}) fusion(bf16[1024,3072]{1,0:T(8,128)(2,1)} %copy.22), kind=kLoop, calls=%fused_computation.6 | loop fusion | flops 12580864 | bytes 6299648 | tf_op jit(solution)/shard_map/reduce_sum | solution.py:57
  87.1 3.8 %fusion.7 = bf16[1024,3072]{1,0:T(8,128)(2,1)S(1)} fusion(bf16[1024,3072]{1,0:T(8,128)(2,1)S(1)} %copy-done.2, f32[3072]{0:T(1024)S(1)} %bitcast.79, f32[3072]{0:T(1024)S(1)} %bitcast.78, f32[1024]{0:T(1024)S(1)} %get-tuple-element.8, f32[1024]{0:T(1024)S(1)} %get-tuple-element.7), kind=kLoop, calls=%fused_computation.11 | loop fusion | flops 18874368 | bytes 12615680 | tf_op jit(solution)/shard_map/convert_element_type | solution.py:32
  95.4 1.0 add_convert_fusion
  96.5 0.8 slice.37
  97.6 31.9 %all-gather.7.cloned.1.call-done = bf16[8192,2,128]{2,0,1:T(8,128)(2,1)} async-done(((bf16[1024,2,128]{2,0,1:T(8,128)(2,1)}), bf16[8192,2,128]{2,0,1:T(8,128)(2,1)}) %all-gather.7.cloned.1.call-update) | async-done | bytes 4194320 | tf_op jit(solution)/shard_map/all_gather | solution.py:73
  129.4 14.7 %multiply_reduce_fusion = (f32[1024]{0:T(1024)S(1)}, f32[1024,8192]{1,0:T(8,128)}) fusion(bf16[8192,2,128]{2,0,1:T(8,128)(2,1)} %all-gather.7.cloned.1.call-done, bf16[1024,3,128]{2,0,1:T(8,128)(2,1)S(1)} %add_convert_fusion), kind=kOutput, calls=%fused_computation.1 | convolution fusion | flops 2164259840 | bytes 35917824 | tf_op jit(solution)/shard_map/dot_general | solution.py:77
  144.1 14.3 %fusion = f32[1024]{0:T(1024)S(1)} fusion(f32[1024,8192]{1,0:T(8,128)} %get-tuple-element.10, f32[1024]{0:T(1024)S(1)} %get-tuple-element.9), kind=kLoop, calls=%fused_computation.2 | loop fusion | flops 25164800 | bytes 33562624 | tf_op jit(solution)/shard_map/reduce_sum | solution.py:79
  158.4 14.2 %fusion.15 = bf16[1024,128]{1,0:T(8,128)(2,1)} fusion(bf16[8192,2,128]{2,0,1:T(8,128)(2,1)S(1)} %copy-done.4, f32[1024,8192]{1,0:T(8,128)} %get-tuple-element.10, f32[1024]{0:T(1024)S(1)} %get-tuple-element.9, f32[1024]{0:T(1024)S(1)} %fusion), kind=kOutput, calls=%fused_computation.21 | convolution fusion | flops 2172911616 | bytes 35921920 | tf_op jit(solution)/shard_map/dot_general | solution.py:80
  172.6 1.2 copy.24
  173.8 6.8 %all-to-all-start = ((bf16[128,16,192]{0,2,1:T(8,128)(2,1)}), bf16[128,16,192]{0,2,1:T(8,128)(2,1)S(1)}, u32[]{:S(2)}, u32[]{:S(2)}) async-start(bf16[128,16,192]{0,2,1:T(8,128)(2,1)} %bitcast.20), calls=%async_computation | async-start | bytes 1572864 | tf_op jit(solution)/shard_map/all_to_all | solution.py:43
  180.6 17.5 %all-to-all-done = bf16[128,16,192]{0,2,1:T(8,128)(2,1)S(1)} async-done(((bf16[128,16,192]{0,2,1:T(8,128)(2,1)}), bf16[128,16,192]{0,2,1:T(8,128)(2,1)S(1)}, u32[]{:S(2)}, u32[]{:S(2)}) %all-to-all-start) | async-done | bytes 786464 | tf_op jit(solution)/shard_map/all_to_all | solution.py:43
  198.2 36.1 %all-gather.9.cloned.1.call-done = bf16[1024,2048]{1,0:T(8,128)(2,1)} async-done(((bf16[1024,128]{1,0:T(8,128)(2,1)}), bf16[1024,2048]{1,0:T(8,128)(2,1)}) %all-gather.9.cloned.1.call-update) | async-done | bytes 4194320 | tf_op jit(solution)/shard_map/all_gather | solution.py:82
  234.3 4.5 %fusion.11 = bf16[1024,192]{0,1:T(8,128)(2,1)} fusion(bf16[1024,2048]{1,0:T(8,128)(2,1)} %all-gather.9.cloned.1.call-done, bf16[1024,192]{0,1:T(8,128)(2,1)S(1)} %copy-done.3, f32[192]{0:T(256)S(1)} %bitcast.83, bf16[128,16,192]{0,2,1:T(8,128)(2,1)S(1)} %all-to-all-done), kind=kOutput, calls=%fused_computation.19 | convolution fusion | flops 806092800 | bytes 5767936 | tf_op jit(solution)/shard_map/dot_general | solution.py:83
  (47 shorter events, 5.4 us)
Async XLA Ops:
  6.5 7.7 %copy-start = (bf16[256,3,192]{0,2,1:T(8,128)(2,1)S(1)}, bf16[256,3,192]{0,2,1:T(8,128)(2,1)}, u32[]{:S(2)}) copy-start(bf16[256,3,192]{0,2,1:T(8,128)(2,1)} %param.11) | copy-start | bytes 884740
  6.5 67.1 %all-gather.5.cloned.1.call-start = ((), (), s32[]{:S(2)}) async-start(), calls=%async_computation.1 | async-start | bytes 6684672 | tf_op jit(solution)/shard_map/all_gather | solution.py:44
  9.9 119.6 %all-gather.7.cloned.1.call-start = ((), (), s32[]{:S(2)}) async-start(), calls=%async_computation.2 | async-start | bytes 4718592 | tf_op jit(solution)/shard_map/all_gather | solution.py:73
  9.9 28.6 %collective-permute-start = (bf16[384,3,128]{2,0,1:T(8,128)(2,1)}, bf16[384,3,128]{2,0,1:T(8,128)(2,1)S(1)}, u32[]{:S(2)}, u32[]{:S(2)}) collective-permute-start(bf16[384,3,128]{2,0,1:T(8,128)(2,1)} %param.12), channel_id=1, source_target_pairs={{0,112},{16,0},{32,16},{48,32},{64,48},{80,64},{96,80},{112,96},{1... | collective-permute-start | bytes 884744 | tf_op jit(solution)/shard_map/ppermute | solution.py:23
  13.5 24.9 %collective-permute-start.1 = (bf16[384,3,128]{2,0,1:T(8,128)(2,1)}, bf16[384,3,128]{2,0,1:T(8,128)(2,1)S(1)}, u32[]{:S(2)}, u32[]{:S(2)}) collective-permute-start(bf16[384,3,128]{2,0,1:T(8,128)(2,1)} %param.12), channel_id=1, source_target_pairs={{0,16},{16,32},{32,48},{48,64},{64,80},{80,96},{96,112},{112,0},{1... | collective-permute-start | bytes 884744 | tf_op jit(solution)/shard_map/ppermute | solution.py:21
  38.4 7.4 %collective-permute-start.3 = (bf16[384,3,128]{2,0,1:T(8,128)(2,1)S(1)}, bf16[384,3,128]{2,0,1:T(8,128)(2,1)S(1)}, u32[]{:S(2)}, u32[]{:S(2)}) collective-permute-start(bf16[384,3,128]{2,0,1:T(8,128)(2,1)S(1)} %collective-permute-done.1), channel_id=1, source_target_pairs={{0,16},{16,32},{32,48},{48,64},{64,80},{80,96},{96,112},{112,0},{1... | collective-permute-start | bytes 884744 | tf_op jit(solution)/shard_map/ppermute | solution.py:21
  38.5 7.5 %collective-permute-start.2 = (bf16[384,3,128]{2,0,1:T(8,128)(2,1)S(1)}, bf16[384,3,128]{2,0,1:T(8,128)(2,1)S(1)}, u32[]{:S(2)}, u32[]{:S(2)}) collective-permute-start(bf16[384,3,128]{2,0,1:T(8,128)(2,1)S(1)} %collective-permute-done), channel_id=1, source_target_pairs={{0,112},{16,0},{32,16},{48,32},{64,48},{80,64},{96,80},{112,96},{1... | collective-permute-start | bytes 884744 | tf_op jit(solution)/shard_map/ppermute | solution.py:23
  45.8 7.4 %collective-permute-start.5 = (bf16[384,3,128]{2,0,1:T(8,128)(2,1)S(1)}, bf16[384,3,128]{2,0,1:T(8,128)(2,1)S(1)}, u32[]{:S(2)}, u32[]{:S(2)}) collective-permute-start(bf16[384,3,128]{2,0,1:T(8,128)(2,1)S(1)} %collective-permute-done.3), channel_id=1, source_target_pairs={{0,16},{16,32},{32,48},{48,64},{64,80},{80,96},{96,112},{112,0},{1... | collective-permute-start | bytes 884744 | tf_op jit(solution)/shard_map/ppermute | solution.py:21
  46.0 48.8 %collective-permute-start.4 = (bf16[384,3,128]{2,0,1:T(8,128)(2,1)S(1)}, bf16[384,3,128]{2,0,1:T(8,128)(2,1)S(1)}, u32[]{:S(2)}, u32[]{:S(2)}) collective-permute-start(bf16[384,3,128]{2,0,1:T(8,128)(2,1)S(1)} %collective-permute-done.2), channel_id=1, source_target_pairs={{0,112},{16,0},{32,16},{48,32},{64,48},{80,64},{96,80},{112,96},{1... | collective-permute-start | bytes 884744 | tf_op jit(solution)/shard_map/ppermute | solution.py:23
  53.2 42.2 %collective-permute-start.6 = (bf16[384,3,128]{2,0,1:T(8,128)(2,1)S(1)}, bf16[384,3,128]{2,0,1:T(8,128)(2,1)S(1)}, u32[]{:S(2)}, u32[]{:S(2)}) collective-permute-start(bf16[384,3,128]{2,0,1:T(8,128)(2,1)S(1)} %collective-permute-done.5), channel_id=1, source_target_pairs={{0,16},{16,32},{32,48},{48,64},{64,80},{80,96},{96,112},{112,0},{1... | collective-permute-start | bytes 884744 | tf_op jit(solution)/shard_map/ppermute | solution.py:21
  82.3 4.8 %copy-start.2 = (bf16[1024,3072]{1,0:T(8,128)(2,1)S(1)}, bf16[1024,3072]{1,0:T(8,128)(2,1)}, u32[]{:S(2)}) copy-start(bf16[1024,3072]{1,0:T(8,128)(2,1)} %copy.22) | copy-start | bytes 18874372
  87.1 3.8 %copy-start.6 = (bf16[384,3,128]{2,0,1:T(8,128)(2,1)S(1)}, bf16[384,3,128]{2,0,1:T(8,128)(2,1)}, u32[]{:S(2)}) copy-start(bf16[384,3,128]{2,0,1:T(8,128)(2,1)} %param.12) | copy-start | bytes 884740
  97.3 136.9 %all-gather.9.cloned.1.call-start = ((), (), s32[]{:S(2)}) async-start(), calls=%async_computation.3 | async-start | bytes 4456448 | tf_op jit(solution)/shard_map/all_gather | solution.py:82
  144.1 14.3 %copy-start.4 = (bf16[8192,2,128]{2,0,1:T(8,128)(2,1)S(1)}, bf16[8192,2,128]{2,0,1:T(8,128)(2,1)}, u32[]{:S(2)}) copy-start(bf16[8192,2,128]{2,0,1:T(8,128)(2,1)} %all-gather.7.cloned.1.call-done) | copy-start | bytes 12582916
  158.4 14.2 %copy-start.5 = (bf16[128,3072]{1,0:T(8,128)(2,1)S(1)}, bf16[128,3072]{1,0:T(8,128)(2,1)}, u32[]{:S(2)}) copy-start(bf16[128,3072]{1,0:T(8,128)(2,1)} %param.13) | copy-start | bytes 2359300
  158.4 75.8 %copy-start.3 = (bf16[1024,192]{0,1:T(8,128)(2,1)S(1)}, bf16[1024,192]{0,1:T(8,128)(2,1)}, u32[]{:S(2)}) copy-start(bf16[1024,192]{0,1:T(8,128)(2,1)} %add_convert_fusion.1) | copy-start | bytes 1179652
  158.4 80.3 %copy-start.1 = (bf16[256,3,192]{0,2,1:T(8,128)(2,1)S(1)}, bf16[256,3,192]{0,2,1:T(8,128)(2,1)}, u32[]{:S(2)}) copy-start(bf16[256,3,192]{0,2,1:T(8,128)(2,1)} %param.11) | copy-start | bytes 884740
  173.8 24.4 %all-to-all-start = ((bf16[128,16,192]{0,2,1:T(8,128)(2,1)}), bf16[128,16,192]{0,2,1:T(8,128)(2,1)S(1)}, u32[]{:S(2)}, u32[]{:S(2)}) async-start(bf16[128,16,192]{0,2,1:T(8,128)(2,1)} %bitcast.20), calls=%async_computation | async-start | bytes 1572864 | tf_op jit(solution)/shard_map/all_to_all | solution.py:43
Sparse Core Ops, SparseCore 0:
  10.0 63.5 all-gather.4
  97.4 31.9 all-gather.6
  172.8 61.4 all-gather.8
